TPU v7x, 512 devices: a whole 4x8x8 slice. The times are simulated.
512 devices in a mesh: req: 64 (over y, x, core), tp: 8 (over z).
Axes of the slice: x: 4, y: 8, z: 8, core: 2. Of those that a mesh axis runs over, the one named last changes fastest.
Arguments:
- hidden: bfloat16 [2048, 5, 2560], P('req', None, 'tp'), may hold values from -6 to 6
- norm_gain: bfloat16 [2560], replicated, may hold values from 0.099609375 to 1.8984375
- query_weight: bfloat16 [2560, 2560], P(None, 'tp'), may hold values from -0.125 to 0.125
- key_value_matrix: bfloat16 [2560, 8, 160], P(None, 'tp'), may hold values from -0.125 to 0.125
- output_weight: bfloat16 [2560, 2560], P('tp'), may hold values from -0.5 to 0.5
- key_value_cache: bfloat16 [2048, 64, 8, 160], P('req', None, 'tp'), as said below
- deal_order: int32 [2048], P('req'), may hold values from 0 to 2047, as said below
- cache_length: int32 [2048], P('req'), may hold values from 1 to 64, as said below
- accepted: int32 [2048], P('req'), may hold values from 1 to 5
Outputs:
- block_output: bfloat16 [2048, 5, 2560], P('req', None, 'tp')
- new_entries: bfloat16 [2048, 5, 8, 160], P('req', None, 'tp')
Inputs may be any that keep to these rules, and one draw needn't show every extreme that they name: deal_order is a permutation of the 2048 requests; slot i lies on index i // 32 of req, and request r arrives on index r // 32. Every index deals at most 1 of its requests to any one index, and exactly 1 to each of 32 indices. Cache entries of slot i at positions from cache_length[i] on are unused. `key_value_cache`: at positions below cache_length[i] the first 80 entries of each head are the keys, already rotated for their positions, and the last 80 the values.
All inputs are finite; a program needn't handle non-finite values.
Results may differ from a plain program's by a relative error of at most 0.0091.
Values may be sent and summed in bfloat16 or wider, within the bound.
No kernel may reach another device: no remote copies, remote signals or barrier semaphores. Data moves between devices by JAX's collectives and lax.ppermute only.
A program may use at most 128 MiB of HBM per device.

v0:
```python
import math
import jax
import jax.numpy as jnp
from jax import lax
from jax.sharding import PartitionSpec as P

HEAD_SIZE = 80
masked_score = -1e30


def rotate(values, positions):
    half_dim = HEAD_SIZE // 2
    frequency = 10000.0 ** (-2.0 * jnp.arange(half_dim, dtype=jnp.float32) / HEAD_SIZE)
    angles = positions.astype(jnp.float32)[..., None] * frequency
    cosine_part = jnp.cos(angles)
    sine_part = jnp.sin(angles)
    first_half = values[..., :half_dim]
    second_half = values[..., half_dim:]
    return jnp.concatenate(
        [
            first_half * cosine_part - second_half * sine_part,
            second_half * cosine_part + first_half * sine_part,
        ],
        axis=-1,
    )


def attend(query_rows, key_value_cache, fresh, cache_length):
    scale = 1.0 / math.sqrt(HEAD_SIZE)
    slot_count = query_rows.shape[0]
    verified = query_rows.shape[1]
    cache_keys = key_value_cache[..., :HEAD_SIZE]
    cache_values = key_value_cache[..., HEAD_SIZE:]
    fresh_keys = fresh[..., :HEAD_SIZE]
    fresh_values = fresh[..., HEAD_SIZE:]
    cache_scores = (
        jnp.einsum("rtghd,rcgd->rghtc", query_rows, cache_keys, preferred_element_type=jnp.float32)
        * scale
    )
    visible = jnp.arange(key_value_cache.shape[1], dtype=jnp.int32)[None, :] < cache_length[:, None]
    cache_scores = jnp.where(visible[:, None, None, None, :], cache_scores, masked_score)
    fresh_scores = (
        jnp.einsum("rtghd,rugd->rghtu", query_rows, fresh_keys, preferred_element_type=jnp.float32)
        * scale
    )
    causal = (
        jnp.arange(verified, dtype=jnp.int32)[:, None]
        >= jnp.arange(verified, dtype=jnp.int32)[None, :]
    )
    fresh_scores = jnp.where(causal[None, None, None, :, :], fresh_scores, masked_score)
    largest = jnp.maximum(jnp.max(cache_scores, axis=-1), jnp.max(fresh_scores, axis=-1))[..., None]
    cache_expos = jnp.exp(cache_scores - largest)
    fresh_expos = jnp.exp(fresh_scores - largest)
    totals = jnp.sum(cache_expos, axis=-1, keepdims=True) + jnp.sum(
        fresh_expos, axis=-1, keepdims=True
    )
    cache_weights = (cache_expos / totals).astype(jnp.bfloat16)
    fresh_weights = (fresh_expos / totals).astype(jnp.bfloat16)
    mixed = jnp.einsum(
        "rghtc,rcgd->rtghd", cache_weights, cache_values, preferred_element_type=jnp.float32
    )
    mixed = mixed + jnp.einsum(
        "rghtu,rugd->rtghd", fresh_weights, fresh_values, preferred_element_type=jnp.float32
    )
    return mixed.astype(jnp.bfloat16).reshape(slot_count, verified, -1)


def body(
    hidden,
    norm_gain,
    query_weight,
    key_value_matrix,
    output_weight,
    key_value_cache,
    deal_order,
    cache_length,
    accepted,
):
    slot_count = deal_order.shape[0]
    verified = hidden.shape[1]
    device_index = lax.axis_index("req")
    my_requests = device_index * slot_count + jnp.arange(slot_count, dtype=jnp.int32)
    piece = lax.all_gather(hidden, "req", axis=0, tiled=True)
    picker = (deal_order[:, None] == jnp.arange(piece.shape[0], dtype=jnp.int32)[None, :]).astype(
        jnp.bfloat16
    )
    dealt_rows = jnp.einsum(
        "in,ntf->itf", picker, piece, preferred_element_type=jnp.float32
    ).astype(jnp.bfloat16)
    features = lax.all_gather(dealt_rows, "tp", axis=2, tiled=True)
    widened = features.astype(jnp.float32)
    variance = jnp.mean(widened * widened, axis=-1, keepdims=True)
    normed = (widened * lax.rsqrt(variance + 1e-05) * norm_gain.astype(jnp.float32)).astype(
        jnp.bfloat16
    )
    heads_here = query_weight.shape[1] // HEAD_SIZE
    groups_here = key_value_matrix.shape[1]
    positions = cache_length[:, None] + jnp.arange(verified, dtype=jnp.int32)[None, :]
    query_rows = jnp.einsum("rtd,de->rte", normed, query_weight, preferred_element_type=jnp.float32)
    query_rows = query_rows.reshape(
        slot_count, verified, groups_here, heads_here // groups_here, HEAD_SIZE
    )
    query_rows = rotate(query_rows, positions[:, :, None, None]).astype(jnp.bfloat16)
    projected = jnp.einsum(
        "rtd,dge->rtge", normed, key_value_matrix, preferred_element_type=jnp.float32
    )
    fresh = jnp.concatenate(
        [rotate(projected[..., :HEAD_SIZE], positions[:, :, None]), projected[..., HEAD_SIZE:]],
        axis=-1,
    ).astype(jnp.bfloat16)
    keep = (jnp.arange(verified, dtype=jnp.int32)[None, :] < accepted[:, None])[:, :, None, None]
    new_entries = jnp.where(keep, fresh, jnp.zeros_like(fresh))
    mixed = attend(query_rows, key_value_cache, fresh, cache_length)
    partial_sum = jnp.einsum(
        "rte,ed->rtd", mixed, output_weight, preferred_element_type=jnp.float32
    )
    out_dealt = lax.psum_scatter(partial_sum, "tp", scatter_dimension=2, tiled=True).astype(
        jnp.bfloat16
    )
    piece_rows = lax.all_gather(out_dealt, "req", axis=0, tiled=True)
    piece_owners = lax.all_gather(deal_order, "req", axis=0, tiled=True)
    picker = (my_requests[:, None] == piece_owners[None, :]).astype(jnp.bfloat16)
    block_output = jnp.einsum(
        "jn,ntf->jtf", picker, piece_rows, preferred_element_type=jnp.float32
    ).astype(jnp.bfloat16)
    return (block_output, new_entries)


def solution(mesh):
    placed = (
        P("req", None, "tp"),
        P(),
        P(None, "tp"),
        P(None, "tp", None),
        P("tp", None),
        P("req", None, "tp", None),
        P("req"),
        P("req"),
        P("req"),
    )
    return jax.shard_map(
        body,
        mesh=mesh,
        in_specs=placed,
        out_specs=(P("req", None, "tp"), P("req", None, "tp", None)),
        check_vma=False,
    )
```

profile of v0, /device:TPU:1, one launch (start us, length us, event | category | flops | bytes accessed | tf_op | source)
XLA Modules:
  0.0 338.5 jit_solution(15841835390689357700)
XLA Ops:
  7.2 0.7 all-gather.3.cloned.1.call-update
  8.0 0.7 convert_element_type.71
  8.7 0.7 add_convert_fusion
  9.4 0.7 iota_compare_fusion.1
  10.7 93.9 %all-gather.3.cloned.1.call-done = bf16[2048,5,320]{2,0,1:T(8,128)(2,1)} async-done(((bf16[32,5,320]{2,0,1:T(8,128)(2,1)}), bf16[2048,5,320]{2,0,1:T(8,128)(2,1)}) %all-gather.3.cloned.1.call-update) | async-done | bytes 6553616 | tf_op jit(solution)/shard_map/all_gather | solution.py:83
  104.6 4.7 %convolution_convert_fusion.1 = bf16[32,5,320]{2,0,1:T(8,128)(2,1)S(1)} fusion(bf16[2048,5,320]{2,0,1:T(8,128)(2,1)} %all-gather.3.cloned.1.call-done, s32[32]{0:T(128)} %param.15), kind=kOutput, calls=%fused_computation.21 | convolution fusion | flops 209831936 | bytes 6656128 | tf_op jit(solution)/shard_map/in,ntf->itf/dot_general | solution.py:87
  109.7 55.1 %all_gather.14 = bf16[32,5,2560]{0,1,2:T(8,128)(2,1)} all-gather(bf16[32,5,320]{0,1,2:T(8,128)(2,1)S(1)} %copy.43), channel_id=1, replica_groups=mesh['req'=64,'tp'=8] {'tp'}, dimensions={2}, use_global_device_ids=true | all-gather | bytes 921600 | tf_op jit(solution)/shard_map/all_gather | solution.py:90
  164.9 4.4 %copy.44 = bf16[32,5,2560]{2,0,1:T(8,128)(2,1)S(1)} copy(bf16[32,5,2560]{0,1,2:T(8,128)(2,1)} %all_gather.14) | data formatting | bytes 1638400 | tf_op jit(solution)/shard_map/all_gather | solution.py:90
  169.5 1.7 convolution_bitcast_fusion.1
  172.3 0.8 fusion.5
  174.1 1.4 fusion.51
  176.8 0.8 convolution_bitcast_fusion
  178.2 0.6 fusion.3
  178.8 5.5 %copy.64 = f32[32,5,2560]{0,1,2:T(8,128)} copy(f32[32,5,2560]{2,0,1:T(8,128)S(1)} %fusion.3) | data formatting | bytes 3276800
  184.3 8.0 %reshape.347 = f32[2560,160]{1,0:T(8,128)} reshape(f32[2560,5,32]{2,1,0:T(8,128)} %bitcast.87) | data formatting | bytes 3276800
  192.4 39.6 %reduce-scatter.4.cloned.1.call-done = f32[320,160]{1,0:T(8,128)} async-done(((f32[2560,160]{1,0:T(8,128)}), f32[320,160]{1,0:T(8,128)}) %reduce-scatter.4.cloned.1.call-update) | async-done | bytes 204816
  232.1 1.2 reshape.348
  233.3 1.0 copy.65
  234.3 1.3 dynamic-slice
  236.5 21.3 %all-reduce = s32[2048]{0:T(1024)S(1)} all-reduce(s32[2048]{0:T(1024)S(1)} %dynamic-update-slice), channel_id=1, replica_groups=mesh['req'=64,'tp'=8] {'req'}, use_global_device_ids=true, to_apply=%add | all-reduce | flops 2048 | bytes 16384
  257.9 1.0 slice.51
  258.9 0.8 fusion.44
  259.7 67.0 %all-gather.5.cloned.1.call-done = bf16[2048,5,320]{2,0,1:T(8,128)(2,1)} async-done(((bf16[32,5,320]{2,0,1:T(8,128)(2,1)}), bf16[2048,5,320]{2,0,1:T(8,128)(2,1)}) %all-gather.5.cloned.1.call-update) | async-done | bytes 6553616 | tf_op jit(solution)/shard_map/all_gather | solution.py:120
  326.7 5.3 %convolution_convert_fusion = bf16[32,5,320]{2,0,1:T(8,128)(2,1)} fusion(bf16[2048,5,320]{2,0,1:T(8,128)(2,1)} %all-gather.5.cloned.1.call-done, s32[2048]{0:T(1024)S(1)} %all-reduce, s32[32]{0:T(128)S(1)} %iota_add_fusion), kind=kOutput, calls=%fused_computation.20 | convolution fusion | flops 209831936 | bytes 6664320 | tf_op jit(solution)/shard_map/jn,ntf->jtf/dot_general | solution.py:123
  (42 shorter events, 5.7 us)
Async XLA Ops:
  7.2 171.1 %copy-start = (bf16[320,2560]{1,0:T(8,128)(2,1)S(1)}, bf16[320,2560]{1,0:T(8,128)(2,1)}, u32[]{:S(2)}) copy-start(bf16[320,2560]{1,0:T(8,128)(2,1)} %param.13) | copy-start | bytes 4915204
  7.2 97.5 %all-gather.3.cloned.1.call-start = ((), (), s32[]{:S(2)}) async-start(), calls=%async_computation.1 | async-start | bytes 7987200 | tf_op jit(solution)/shard_map/all_gather | solution.py:83
  7.9 224.2 %reduce-scatter.4.cloned.1.call-start = ((), (), s32[]{:S(2)}) async-start(), calls=%async_computation.3 | async-start | bytes 2949120
  169.2 3.0 copy-start.4
  171.2 0.7 copy-start.1
  173.5 1.9 copy-start.2
  192.4 43.9 %copy-start.3 = (s32[32]{0:T(128)S(1)}, s32[32]{0:T(128)}, u32[]{:S(2)}) copy-start(s32[32]{0:T(128)} %param.15) | copy-start | bytes 388
  192.4 65.5 %copy-start.5 = (s32[32]{0:T(128)S(1)}, s32[32]{0:T(128)}, u32[]{:S(2)}) copy-start(s32[32]{0:T(128)} %param.17) | copy-start | bytes 388
  192.4 134.3 %all-gather.5.cloned.1.call-start = ((), (), s32[]{:S(2)}) async-start(), calls=%async_computation.2 | async-start | bytes 7987200 | tf_op jit(solution)/shard_map/all_gather | solution.py:120
Sparse Core Ops, SparseCore 0:
  11.3 93.2 all-gather.2
  192.5 39.5 reduce-scatter.3
  235.9 90.6 all-gather.4
where the time goes:
time: 339 us; the launch traced here: 338 us
  waiting for transfers between devices  201 us (59%)
  blocking collectives  76.4 us (23%)
  local copies, waits for them, and re-layouts  24.5 us (7%)
  matrix products  16.2 us (5%)
  between operations  14.6 us (4%)
  other arithmetic  5.35 us (2%)
    all_gather x1, waiting for transfers between devices, body(): piece = lax.all_gather(hidden, 'req', axis=0, tiled=True)  93.9 us
    all_gather x1, waiting for transfers between devices, body(): piece_rows = lax.all_gather(out_dealt, 'req', axis=0, tiled=True)  67 us
    all_gather x1, blocking collectives, body(): features = lax.all_gather(dealt_rows, 'tp', axis=2, tiled=True)  55.1 us
    unnamed x4, waiting for transfers between devices  40.3 us
    unnamed x1, blocking collectives  21.3 us
    unnamed x19, local copies, waits for them, and re-layouts  17.9 us
  transfers between devices with their start and end apart: 3, of which 3 were waited for; matrix products, arithmetic and copies ran while one was open for 2% of the time, Pallas kernels for 0%

commit v1 on v0

--- a/solution.py
+++ b/solution.py
@@ -6,6 +6,18 @@
 
 HEAD_SIZE = 80
 masked_score = -1e30
+
+
+def hold_the_records(sheet):
+    group_axis = "req"
+    parts_out = lax.all_to_all(
+        jnp.concatenate([sheet for _ in range(lax.axis_size(group_axis))], 0),
+        group_axis,
+        0,
+        0,
+        tiled=True,
+    )
+    return parts_out
 
 
 def rotate(values, positions):
@@ -117,7 +129,7 @@
     out_dealt = lax.psum_scatter(partial_sum, "tp", scatter_dimension=2, tiled=True).astype(
         jnp.bfloat16
     )
-    piece_rows = lax.all_gather(out_dealt, "req", axis=0, tiled=True)
+    piece_rows = hold_the_records(out_dealt)
     piece_owners = lax.all_gather(deal_order, "req", axis=0, tiled=True)
     picker = (my_requests[:, None] == piece_owners[None, :]).astype(jnp.bfloat16)
     block_output = jnp.einsum(

time: 339 us -> 594 us (1.75)
  blocking collectives: 76.4 us -> 333 us
  waiting for transfers between devices: 201 us -> 135 us
  local copies, waits for them, and re-layouts: 24.5 us -> 65.9 us
  starting transfers between devices: 0.12 us -> 14.6 us
    unnamed x1, blocking collectives: 21.3 us -> 278 us
    all_gather x1 -> x0, waiting for transfers between devices: 67 us -> none  [body(): piece_rows = lax.all_gather(out_dealt, 'req', axis=0, tiled=True)]
    concatenate x0 -> x2, local copies, waits for them, and re-layouts: none -> 40.6 us  [hold_the_records(): jnp.concatenate([sheet for _ in range(lax.axis_size(group_axis))], 0)]
    all_to_all x0 -> x1, starting transfers between devices: none -> 14.5 us  [hold_the_records(): lax.all_to_all(jnp.concatenate([sheet for _ in range(lax.axis_size(group_...]
    unnamed x19 -> x80, local copies, waits for them, and re-layouts: 17.9 us -> 18.7 us
    unnamed x4 -> x3, waiting for transfers between devices: 40.3 us -> 40.7 us
  transfers between devices with their start and end apart: 3 -> 3, of which waited for: 3 -> 2; matrix products, arithmetic and copies ran while one was open for 2% -> 1% of each run, Pallas kernels for 0% -> 0%
where the time goes in v1:
time: 594 us; the launch traced here: 591 us
  blocking collectives  333 us (56%)
  waiting for transfers between devices  135 us (23%)
  local copies, waits for them, and re-layouts  65.9 us (11%)
  matrix products  21.5 us (4%)
  between operations  15.4 us (3%)
  starting transfers between devices  14.6 us (2%)
    unnamed x1, blocking collectives  278 us
    all_gather x1, waiting for transfers between devices, body(): piece = lax.all_gather(hidden, 'req', axis=0, tiled=True)  93.9 us
    all_gather x1, blocking collectives, body(): features = lax.all_gather(dealt_rows, 'tp', axis=2, tiled=True)  55.1 us
    unnamed x3, waiting for transfers between devices  40.7 us
    concatenate x2, local copies, waits for them, and re-layouts, hold_the_records(): jnp.concatenate([sheet for _ in range(lax.axis_size(group_axis))], 0)  40.6 us
    unnamed x80, local copies, waits for them, and re-layouts  18.7 us
    all_to_all x1, starting transfers between devices, hold_the_records(): lax.all_to_all(jnp.concatenate([sheet for _ in range(lax.axis_size(group_...  14.5 us
  transfers between devices with their start and end apart: 3, of which 2 were waited for; matrix products, arithmetic and copies ran while one was open for 1% of the time, Pallas kernels for 0%

profile of v1, /device:TPU:1, one launch (start us, length us, event | category | flops | bytes accessed | tf_op | source)
XLA Modules:
  0.0 590.8 jit_solution(13840675870241050126)
XLA Ops:
  7.2 0.7 all-gather.2.cloned.1.call-update
  8.0 0.7 convert_element_type.71
  8.7 0.7 add_convert_fusion
  9.4 0.7 iota_compare_fusion.1
  10.7 93.9 %all-gather.2.cloned.1.call-done = bf16[2048,5,320]{2,0,1:T(8,128)(2,1)} async-done(((bf16[32,5,320]{2,0,1:T(8,128)(2,1)}), bf16[2048,5,320]{2,0,1:T(8,128)(2,1)}) %all-gather.2.cloned.1.call-update) | async-done | bytes 6553616 | tf_op jit(solution)/shard_map/all_gather | solution.py:95
  104.6 4.7 convolution_convert_fusion
  109.7 55.1 %all_gather.11 = bf16[32,5,2560]{0,1,2:T(8,128)(2,1)} all-gather(bf16[32,5,320]{0,1,2:T(8,128)(2,1)S(1)} %copy.60), channel_id=1, replica_groups=mesh['req'=64,'tp'=8] {'tp'}, dimensions={2}, use_global_device_ids=true | all-gather | bytes 921600 | tf_op jit(solution)/shard_map/all_gather | solution.py:102
  164.9 4.4 copy.61
  169.5 1.6 convolution_bitcast_fusion.1
  172.1 2.2 fusion.7
  175.4 1.4 fusion.56
  176.7 1.6 fusion.55
  179.1 1.8 convolution_bitcast_fusion
  182.1 5.5 copy.83
  187.6 8.0 %reshape.347 = f32[2560,160]{1,0:T(8,128)} reshape(f32[2560,5,32]{2,1,0:T(8,128)} %bitcast.86) | data formatting | bytes 3276800
  195.7 40.0 %reduce-scatter.4.cloned.1.call-done = f32[320,160]{1,0:T(8,128)} async-done(((f32[2560,160]{1,0:T(8,128)}), f32[320,160]{1,0:T(8,128)}) %reduce-scatter.4.cloned.1.call-update) | async-done | bytes 204816
  235.7 1.2 reshape.348
  239.1 40.5 %copy.71 = bf16[2048,5,320]{2,1,0:T(8,128)(2,1)} copy(bf16[2048,5,320]{2,0,1:T(8,128)(2,1)S(1)} %constant_dynamic-update-slice_fusion) | data formatting | bytes 13107200 | tf_op jit(solution)/shard_map/concatenate | solution.py:14
  279.7 14.5 %all-to-all-start = ((bf16[2048,5,320]{2,1,0:T(8,128)(2,1)}), bf16[2048,5,320]{2,1,0:T(8,128)(2,1)}, u32[]{:S(2)}, u32[]{:S(2)}) async-start(bf16[2048,5,320]{2,1,0:T(8,128)(2,1)} %copy.71), calls=%async_computation | async-start | bytes 25165824 | tf_op jit(solution)/shard_map/all_to_all | solution.py:13
  294.2 1.4 dynamic-slice
  296.6 278.3 %all-reduce = s32[2048]{0:T(1024)S(1)} all-reduce(s32[2048]{0:T(1024)S(1)} %dynamic-update-slice), channel_id=1, replica_groups=mesh['req'=64,'tp'=8] {'req'}, use_global_device_ids=true, to_apply=%add | all-reduce | flops 2048 | bytes 16384
  574.9 1.0 slice.51
  575.9 0.8 fusion.49
  576.7 7.3 %fusion.16 = bf16[32,5,320]{2,0,1:T(8,128)(2,1)} fusion(bf16[2048,5,320]{2,1,0:T(8,128)(2,1)} %all-to-all-done, s32[2048]{0:T(1024)S(1)} %all-reduce, s32[32]{0:T(128)S(1)} %iota_add_fusion), kind=kOutput, calls=%fused_computation.22 | convolution fusion | flops 209831936 | bytes 6664320 | tf_op jit(solution)/shard_map/jn,ntf->jtf/dot_general | solution.py:135
  (104 shorter events, 7.4 us)
Async XLA Ops:
  7.2 174.4 %copy-start = (bf16[320,2560]{1,0:T(8,128)(2,1)S(1)}, bf16[320,2560]{1,0:T(8,128)(2,1)}, u32[]{:S(2)}) copy-start(bf16[320,2560]{1,0:T(8,128)(2,1)} %param.13) | copy-start | bytes 4915204
  7.2 97.5 %all-gather.2.cloned.1.call-start = ((), (), s32[]{:S(2)}) async-start(), calls=%async_computation.2 | async-start | bytes 7987200 | tf_op jit(solution)/shard_map/all_gather | solution.py:95
  7.9 227.7 %reduce-scatter.4.cloned.1.call-start = ((), (), s32[]{:S(2)}) async-start(), calls=%async_computation.3 | async-start | bytes 2949120
  171.1 0.7 copy-start.2
  279.7 16.6 %copy-start.3 = (s32[32]{0:T(128)S(1)}, s32[32]{0:T(128)}, u32[]{:S(2)}) copy-start(s32[32]{0:T(128)} %param.15) | copy-start | bytes 388
  279.7 295.2 %copy-start.4 = (s32[32]{0:T(128)S(1)}, s32[32]{0:T(128)}, u32[]{:S(2)}) copy-start(s32[32]{0:T(128)} %param.17) | copy-start | bytes 388
  279.7 297.0 %all-to-all-start = ((bf16[2048,5,320]{2,1,0:T(8,128)(2,1)}), bf16[2048,5,320]{2,1,0:T(8,128)(2,1)}, u32[]{:S(2)}, u32[]{:S(2)}) async-start(bf16[2048,5,320]{2,1,0:T(8,128)(2,1)} %copy.71), calls=%async_computation | async-start | bytes 25165824 | tf_op jit(solution)/shard_map/all_to_all | solution.py:13
  294.2 289.7 %copy-start.1 = (bf16[320,2560]{1,0:T(8,128)(2,1)S(1)}, bf16[320,2560]{1,0:T(8,128)(2,1)}, u32[]{:S(2)}) copy-start(bf16[320,2560]{1,0:T(8,128)(2,1)} %param.13) | copy-start | bytes 4915204
Sparse Core Ops, SparseCore 0:
  11.3 93.2 all-gather.1
  195.8 39.8 reduce-scatter.3
